TPU v7x, 256 devices: a whole 4x4x8 slice. The times are simulated.
256 devices in a mesh: facet: 8 (over z), chan: 32 (over y, x, core).
Axes of the slice: x: 4, y: 4, z: 8, core: 2. Of those that a mesh axis runs over, the one named last changes fastest.
Arguments:
- sky_image: float32 [256, 32, 4096], P('chan', 'facet'), may hold values from -100 to 100
- dual_field: float32 [256, 32, 4096], P(None, 'facet', 'chan'), may hold values from -100 to 100
- sketch_matrix: bfloat16 [32, 4096, 128], P('facet', 'chan'), may hold values from -0.046875 to 0.046875
- grid_tiles: float32 [256, 4, 128, 128], P('chan'), may hold values from -0.5 to 0.5
- freq_block: int32 [256, 4], P('chan'), may hold values from 0 to 31
- vis_block: int32 [256, 4], P('chan'), may hold values from 0 to 3
- vis_data: float32 [256, 2, 32, 4, 128], P('chan', None, 'facet'), may hold values from -6 to 6
Outputs:
- new_image: float32 [256, 32, 4096], P('chan', 'facet')
- new_dual: float32 [256, 32, 4096], P(None, 'facet', 'chan')
All inputs are finite; a program needn't handle non-finite values.
Results may differ from a plain program's by a relative error of at most 0.0003.
Values sent between devices are 32-bit elements; how exact they have to be, the bound alone decides.
No kernel may reach another device: no remote copies, remote signals or barrier semaphores. Data moves between devices by JAX's collectives and lax.ppermute only.
A program may use at most 128 MiB of HBM per device.

v0:
```python
import math
import jax
import jax.numpy as jnp
from jax import lax
from jax.sharding import PartitionSpec as P

SIGN_ITERS = 12
ROOT_ITERS = 14
step_primal = 0.4
smooth_weight = 0.25
step_dual = 0.5
shrink_ratio = 0.25


def padded_2(block, sides, width):
    for axis, dim in sides:
        count = lax.axis_size(axis)
        forward = [(i, i + 1) for i in range(count - 1)]
        backward = [(target, source) for source, target in forward]
        low = lax.ppermute(
            lax.slice_in_dim(block, block.shape[dim] - width, None, axis=dim), axis, forward
        )
        high = lax.ppermute(lax.slice_in_dim(block, 0, width, axis=dim), axis, backward)
        block = jnp.concatenate([low, block, high], axis=dim)
    return block


def matmul_hi(first_mat, second_mat):
    return jnp.dot(first_mat, second_mat, precision=lax.Precision.HIGHEST)


def shrink_matrix(gram_mat):
    order_n = gram_mat.shape[0]
    identity = jnp.eye(order_n, dtype=gram_mat.dtype)
    thresh_sq = shrink_ratio * jnp.trace(gram_mat) / order_n
    shifted = gram_mat - thresh_sq * identity
    signum = shifted / jnp.sqrt(jnp.sum(shifted * shifted))

    def sign_step(turn_no, current):
        return 1.5 * current - 0.5 * matmul_hi(matmul_hi(current, current), current)

    signum = lax.fori_loop(0, SIGN_ITERS, sign_step, signum)
    keeper = 0.5 * (identity + signum)
    floored = 0.5 * (gram_mat + thresh_sq * identity + matmul_hi(shifted, signum))
    scale_c = jnp.sqrt(jnp.sum(floored * floored))

    def root_step(turn_no, state_pair):
        root_iter, inv_iter = state_pair
        step_mat = 0.5 * (3.0 * identity - matmul_hi(inv_iter, root_iter))
        return (matmul_hi(root_iter, step_mat), matmul_hi(step_mat, inv_iter))

    root_iter, inv_iter = lax.fori_loop(0, ROOT_ITERS, root_step, (floored / scale_c, identity))
    inv_root = inv_iter / jnp.sqrt(scale_c)
    return matmul_hi(keeper, identity - jnp.sqrt(thresh_sq) * inv_root)


def basis_from(sketch):
    lower_fac = jnp.linalg.cholesky(matmul_hi(sketch.T, sketch))
    return jax.scipy.linalg.solve_triangular(lower_fac, sketch.T, lower=True).T


def phase_pair(count_a, count_b, period):
    first_idx = lax.broadcasted_iota(jnp.int32, (count_a, count_b), 0)
    second_idx = lax.broadcasted_iota(jnp.int32, (count_a, count_b), 1)
    angle_grid = 2.0 * math.pi / period * (first_idx * second_idx % period).astype(jnp.float32)
    return (jnp.cos(angle_grid), jnp.sin(angle_grid))


def spectrum_tables(width, block):
    blocks_n = width // block
    cos_a, sin_a = phase_pair(blocks_n, blocks_n, blocks_n)
    cos_b, sin_b = phase_pair(block, block, block)
    cos_t, sin_t = phase_pair(blocks_n, block, width)
    return (cos_a, sin_a, cos_b, sin_b, cos_t, sin_t)


def forward_rows(rows_img, tables, block):
    cos_a, sin_a, cos_b, sin_b, cos_t, sin_t = tables
    row_count, width = rows_img.shape
    blocks_n = width // block
    hi = lax.Precision.HIGHEST
    blocks = rows_img.reshape(row_count, blocks_n, block)
    part_re = jnp.einsum("kn,bnm->bkm", cos_a, blocks, precision=hi)
    part_im = -jnp.einsum("kn,bnm->bkm", sin_a, blocks, precision=hi)
    turned_re = (part_re * cos_t + part_im * sin_t).reshape(-1, block)
    turned_im = (part_im * cos_t - part_re * sin_t).reshape(-1, block)
    ortho_scale = 1.0 / math.sqrt(width)
    spec_re = (matmul_hi(turned_re, cos_b) + matmul_hi(turned_im, sin_b)) * ortho_scale
    spec_im = (matmul_hi(turned_im, cos_b) - matmul_hi(turned_re, sin_b)) * ortho_scale
    return (
        spec_re.reshape(row_count, blocks_n, block),
        spec_im.reshape(row_count, blocks_n, block),
    )


def adjoint_rows(spec_re, spec_im, tables):
    cos_a, sin_a, cos_b, sin_b, cos_t, sin_t = tables
    row_count, blocks_n, block = spec_re.shape
    hi = lax.Precision.HIGHEST
    flat_re = spec_re.reshape(-1, block)
    flat_im = spec_im.reshape(-1, block)
    back_re = (matmul_hi(flat_re, cos_b) - matmul_hi(flat_im, sin_b)).reshape(
        row_count, blocks_n, block
    )
    back_im = (matmul_hi(flat_im, cos_b) + matmul_hi(flat_re, sin_b)).reshape(
        row_count, blocks_n, block
    )
    turn_re = back_re * cos_t - back_im * sin_t
    turn_im = back_re * sin_t + back_im * cos_t
    rows_out = jnp.einsum("kn,bkm->bnm", cos_a, turn_re, precision=hi) - jnp.einsum(
        "kn,bkm->bnm", sin_a, turn_im, precision=hi
    )
    width = blocks_n * block
    return rows_out.reshape(row_count, width) * (1.0 / math.sqrt(width))


def data_gradient(sky_image, grid_tiles, freq_block, vis_block, vis_data):
    chan_count, row_count, width = sky_image.shape
    block = grid_tiles.shape[2]
    blocks_n = width // block
    hi = lax.Precision.HIGHEST
    tables = spectrum_tables(width, block)
    columns = lax.all_to_all(sky_image, "facet", split_axis=2, concat_axis=1, tiled=True)
    all_rows = columns.shape[1]
    cos_c, sin_c = phase_pair(all_rows, all_rows, all_rows)
    column_scale = 1.0 / math.sqrt(all_rows)
    column_re = jnp.einsum("pq,cqn->cpn", cos_c, columns, precision=hi) * column_scale
    column_im = -jnp.einsum("pq,cqn->cpn", sin_c, columns, precision=hi) * column_scale
    column_spec = jnp.stack([column_re, column_im], 1)
    row_spec = lax.all_to_all(column_spec, "facet", split_axis=2, concat_axis=3, tiled=True)
    four_re, four_im = forward_rows(
        row_spec.reshape(chan_count * 2 * row_count, width), tables, block
    )
    four_re = four_re.reshape(chan_count, 2, row_count, blocks_n, block)
    four_im = four_im.reshape(chan_count, 2, row_count, blocks_n, block)
    spec_re = four_re[:, 0] - four_im[:, 1]
    spec_im = four_im[:, 0] + four_re[:, 1]
    spectra = jnp.stack([spec_re, spec_im], 1)
    pick_onehot = jax.nn.one_hot(freq_block, blocks_n, dtype=jnp.float32)
    place_onehot = jax.nn.one_hot(vis_block, vis_data.shape[3], dtype=jnp.float32)
    chosen = jnp.einsum("ctb,cxrbk->cxtrk", pick_onehot, spectra, precision=hi)
    products = jnp.einsum("cxtrk,ctkm->cxtrm", chosen, grid_tiles, precision=hi)
    predicted = jnp.einsum("ctv,cxtrm->cxrvm", place_onehot, products, precision=hi)
    residual = predicted - vis_data
    spread = jnp.einsum("ctv,cxrvm->cxtrm", place_onehot, residual, precision=hi)
    pulled = jnp.einsum("cxtrm,ctkm->cxtrk", spread, grid_tiles, precision=hi)
    back_spec = jnp.einsum("ctb,cxtrk->cxrbk", pick_onehot, pulled, precision=hi)
    back_re = back_spec[:, 0].reshape(-1, blocks_n, block)
    back_im = back_spec[:, 1].reshape(-1, blocks_n, block)
    inverted = adjoint_rows(
        jnp.concatenate([back_re, back_im], 0), jnp.concatenate([back_im, -back_re], 0), tables
    )
    inverted = jnp.swapaxes(inverted.reshape(2, chan_count, row_count, width), 0, 1)
    spatial = lax.all_to_all(inverted, "facet", split_axis=3, concat_axis=2, tiled=True)
    gradient_cols = (
        jnp.einsum("pq,cpn->cqn", cos_c, spatial[:, 0], precision=hi)
        - jnp.einsum("pq,cpn->cqn", sin_c, spatial[:, 1], precision=hi)
    ) * column_scale
    return lax.all_to_all(gradient_cols, "facet", split_axis=1, concat_axis=2, tiled=True)


def take_sketch(pixels, sketch_rows):
    return jnp.einsum("crw,rwk->ck", pixels, sketch_rows, precision=lax.Precision.HIGHEST)


def project_rows(basis_mat, pixels):
    return jnp.einsum("ck,crw->krw", basis_mat, pixels, precision=lax.Precision.HIGHEST)


def on_device(sky_image, dual_field, sketch_matrix, grid_tiles, freq_block, vis_block, vis_data):
    hi = lax.Precision.HIGHEST
    dual_chan = lax.all_to_all(dual_field, "chan", split_axis=0, concat_axis=2, tiled=True)
    padded = padded_2(sky_image, (("facet", 1),), 1)
    gradient = data_gradient(sky_image, grid_tiles, freq_block, vis_block, vis_data)
    smooth = 2.0 * sky_image - padded[:, :-2] - padded[:, 2:]
    new_image = sky_image - step_primal * (gradient + smooth_weight * smooth + dual_chan)
    merged = dual_chan + step_dual * (2.0 * new_image - sky_image)
    sketch_rows = sketch_matrix.astype(jnp.float32)
    pixels = lax.all_to_all(merged, "chan", split_axis=2, concat_axis=0, tiled=True)
    sketch = lax.psum(take_sketch(pixels, sketch_rows), "chan")
    basis_mat = basis_from(sketch)
    coords = project_rows(basis_mat, pixels)
    gram_mat = lax.psum(jnp.einsum("krw,jrw->kj", coords, coords, precision=hi), "chan")
    shrink = shrink_matrix(gram_mat)
    new_dual = pixels - jnp.einsum(
        "ck,krw->crw", matmul_hi(basis_mat, shrink), coords, precision=hi
    )
    return (new_image, new_dual)


def solution(mesh):
    placed = (
        P("chan", "facet", None),
        P(None, "facet", "chan"),
        P("facet", "chan", None),
        P("chan", None, None, None),
        P("chan", None),
        P("chan", None),
        P("chan", None, "facet", None, None),
    )
    return jax.shard_map(
        on_device,
        mesh=mesh,
        in_specs=placed,
        out_specs=(P("chan", "facet", None), P(None, "facet", "chan")),
        check_vma=False,
    )
```

profile of v0, /device:TPU:1, one launch (start us, length us, event | category | flops | bytes accessed | tf_op | source)
XLA Modules:
  0.0 629.0 jit_solution(11363027889808603613)
XLA Ops:
  7.2 6.9 %copy.95 = f32[8,4,4096]{0,1,2:T(4,128)} copy(f32[8,4,4096]{2,1,0:T(4,128)} %param.11) | data formatting | bytes 1048576 | tf_op args[0]
  14.1 11.4 %reshape.86 = f32[8,1,16384]{2,1,0:T(1,128)S(1)} reshape(f32[4096,4,8]{2,1,0:T(4,128)} %bitcast.218) | data formatting | bytes 1048576
  25.5 25.4 %all_to_all.105 = f32[8,1,16384]{2,1,0:T(1,128)S(1)} all-to-all(f32[8,1,16384]{2,1,0:T(1,128)S(1)} %reshape.86), channel_id=1, replica_groups=mesh['facet'=8,'chan'=32] {'facet'}, dimensions={0} | all-to-all | bytes 1048576 | tf_op jit(solution)/shard_map/all_to_all | solution.py:123
  53.3 13.1 %reshape.87 = f32[4096,4,8]{2,1,0:T(4,128)} reshape(f32[8,16384]{1,0:T(8,128)S(1)} %reduce.6) | data formatting | bytes 1048576
  66.4 6.7 %copy.96 = f32[8,4,8,512]{3,1,2,0:T(4,128)S(1)} copy(f32[8,4,8,512]{0,1,3,2:T(4,128)} %bitcast.215) | data formatting | bytes 1048576 | tf_op jit(solution)/shard_map/all_to_all | solution.py:123
  80.4 28.5 %all-to-all-done.1 = f32[8,2,32,512]{3,0,1,2:T(8,128)S(1)} async-done(((f32[8,2,32,512]{3,0,1,2:T(8,128)}), f32[8,2,32,512]{3,0,1,2:T(8,128)S(1)}, u32[]{:S(2)}, u32[]{:S(2)}) %all-to-all-start.1) | async-done | bytes 1048608 | tf_op jit(solution)/shard_map/all_to_all | solution.py:130
  135.1 11.1 %copy.110 = f32[2,8,4,4096]{1,2,0,3:T(4,128)} copy(f32[2,8,4,4096]{3,2,1,0:T(4,128)S(1)} %mul.315) | data formatting | bytes 2097152 | tf_op jit(solution)/shard_map/mul | solution.py:114
  146.2 14.5 %bitcast_bitcast_fusion = f32[4096,2,4,8]{3,2,1,0:T(4,128)} fusion(f32[2,8,4,4096]{1,2,0,3:T(4,128)} %copy.110), kind=kLoop, calls=%fused_computation.239 | loop fusion | bytes 2097152
  160.7 21.3 %reshape.88 = f32[8,1,32768]{2,1,0:T(1,128)S(1)} reshape(f32[4096,2,4,8]{3,2,1,0:T(4,128)} %bitcast_bitcast_fusion) | data formatting | bytes 2097152
  182.0 30.5 %all_to_all.106 = f32[8,1,32768]{2,1,0:T(1,128)S(1)} all-to-all(f32[8,1,32768]{2,1,0:T(1,128)S(1)} %reshape.88), channel_id=1, replica_groups=mesh['facet'=8,'chan'=32] {'facet'}, dimensions={0} | all-to-all | bytes 2097152 | tf_op jit(solution)/shard_map/all_to_all | solution.py:154
  215.7 25.6 %reshape.89 = f32[4096,2,4,8]{3,2,1,0:T(4,128)} reshape(f32[8,32768]{1,0:T(8,128)S(1)} %reduce.7) | data formatting | bytes 2097152
  241.3 13.2 %copy.111 = f32[8,2,4,8,512]{4,2,3,0,1:T(4,128)S(1)} copy(f32[8,2,4,8,512]{0,2,1,4,3:T(4,128)} %bitcast.214) | data formatting | bytes 2097152 | tf_op jit(solution)/shard_map/all_to_all | solution.py:154
  261.1 16.0 %all-to-all-done.3 = f32[8,32,512]{2,0,1:T(8,128)S(1)} async-done(((f32[8,32,512]{2,0,1:T(8,128)}), f32[8,32,512]{2,0,1:T(8,128)S(1)}, u32[]{:S(2)}, u32[]{:S(2)}) %all-to-all-start.3) | async-done | bytes 524320 | tf_op jit(solution)/shard_map/all_to_all | solution.py:159
  277.2 9.2 %all-to-all-start.4 = ((f32[256,4,128]{2,1,0:T(4,128)}), f32[256,4,128]{2,1,0:T(4,128)S(1)}, u32[]{:S(2)}, u32[]{:S(2)}) async-start(f32[256,4,128]{2,1,0:T(4,128)} %param.12), calls=%async_computation.4 | async-start | bytes 1048576 | tf_op jit(solution)/shard_map/all_to_all | solution.py:172
  298.3 5.9 copy.122
  304.2 11.4 %reshape.90 = f32[32,1,4096]{2,1,0:T(1,128)S(1)} reshape(f32[4096,4,8]{2,1,0:T(4,128)} %bitcast.216) | data formatting | bytes 1048576
  315.6 17.2 %all_to_all.107 = f32[32,1,4096]{2,1,0:T(1,128)S(1)} all-to-all(f32[32,1,4096]{2,1,0:T(1,128)S(1)} %reshape.90), channel_id=1, replica_groups=mesh['facet'=8,'chan'=32] {'chan'}, dimensions={0} | all-to-all | bytes 1048576 | tf_op jit(solution)/shard_map/all_to_all | solution.py:179
  334.7 11.3 %reshape.91 = f32[4096,4,8]{2,1,0:T(4,128)} reshape(f32[32,4096]{1,0:T(8,128)S(1)} %reduce.8) | data formatting | bytes 1048576
  346.0 6.7 %copy.123 = f32[8,4,32,128]{3,0,2,1:T(8,128)S(1)} copy(f32[8,4,32,128]{0,1,3,2:T(4,128)} %bitcast.217) | data formatting | bytes 1048576 | tf_op jit(solution)/shard_map/all_to_all | solution.py:179
  353.9 105.1 %all-reduce.3.cloned.1.call-done = f32[256,128]{1,0:T(8,128)} async-done(((f32[256,128]{1,0:T(8,128)}), f32[256,128]{1,0:T(8,128)}) %all-reduce.3.cloned.1.call-update) | async-done | bytes 131088 | tf_op jit(solution)/shard_map/psum | solution.py:180
  460.4 11.7 %cholesky.22 = f32[128,128]{1,0:T(8,128)S(1)} custom-call(f32[128,128]{1,0:T(8,128)S(1)} %fusion.62), custom_call_target="Cholesky" | custom-call | tf_op jit(solution)/shard_map/jit(cholesky)/cholesky | solution.py:58
  473.5 9.8 %custom-call.7 = f32[1,128,128]{1,2,0:T(8,128)S(1)} custom-call(f32[1,128,128]{2,1,0:T(8,128)S(1)} %fusion.56), custom_call_target="InvertDiagBlocksLowerTriangular" | custom-call | tf_op jit(solution)/shard_map/jit(_solve_triangular)/triangular_solve | solution.py:59
  487.1 106.4 %all-reduce.5.cloned.1.call-done = f32[128,128]{1,0:T(8,128)} async-done(((f32[128,128]{1,0:T(8,128)}), f32[128,128]{1,0:T(8,128)}) %all-reduce.5.cloned.1.call-update) | async-done | bytes 65552 | tf_op jit(solution)/shard_map/psum | solution.py:183
  607.1 11.4 %while.24 = (s32[]{:T(128)}, f32[128,128]{0,1:T(8,128)S(1)}, f32[128,128]{1,0:T(8,128)S(1)}, s32[]{:T(128)}) while((s32[]{:T(128)}, f32[128,128]{0,1:T(8,128)S(1)}, f32[128,128]{1,0:T(8,128)S(1)}, s32[]{:T(128)}) %tuple.57), condition=%wide.region_10.11_spmd.clone, body=%wide.region_9.10_spmd.clone.sunk | while | flops 75563008 | bytes 852021 | solution.py:52
  (201 shorter events, 97.1 us)
Async XLA Ops:
  7.2 112.7 %copy-start = (f32[8,4,128,128]{3,2,1,0:T(8,128)S(1)}, f32[8,4,128,128]{3,2,1,0:T(8,128)}, u32[]{:S(2)}) copy-start(f32[8,4,128,128]{3,2,1,0:T(8,128)} %param.14) | copy-start | bytes 6291460
  66.4 13.8 %copy-start.6 = (s32[8,4]{0,1:T(4,128)S(1)}, s32[8,4]{0,1:T(4,128)}, u32[]{:S(2)}) copy-start(s32[8,4]{0,1:T(4,128)} %param.15) | copy-start | bytes 388
  66.4 13.9 %copy-start.7 = (s32[8,4]{0,1:T(4,128)S(1)}, s32[8,4]{0,1:T(4,128)}, u32[]{:S(2)}) copy-start(s32[8,4]{0,1:T(4,128)} %param.16) | copy-start | bytes 388
  76.4 32.5 %all-to-all-start.1 = ((f32[8,2,32,512]{3,0,1,2:T(8,128)}), f32[8,2,32,512]{3,0,1,2:T(8,128)S(1)}, u32[]{:S(2)}, u32[]{:S(2)}) async-start(f32[8,2,32,512]{3,0,1,2:T(8,128)} %copy.99), calls=%async_computation.1 | async-start | bytes 2097152 | tf_op jit(solution)/shard_map/all_to_all | solution.py:130
  114.2 7.5 %copy-start.4 = (f32[8,2,4,4,128]{4,3,2,1,0:T(4,128)S(1)}, f32[8,2,4,4,128]{4,3,2,1,0:T(4,128)}, u32[]{:S(2)}) copy-start(f32[8,2,4,4,128]{4,3,2,1,0:T(4,128)} %param.17) | copy-start | bytes 393220
  241.3 19.6 %copy-start.2 = (f32[8,4,4096]{2,1,0:T(4,128)S(1)}, f32[8,4,4096]{2,1,0:T(4,128)}, u32[]{:S(2)}) copy-start(f32[8,4,4096]{2,1,0:T(4,128)} %param.11) | copy-start | bytes 1572868
  257.3 19.9 %all-to-all-start.3 = ((f32[8,32,512]{2,0,1:T(8,128)}), f32[8,32,512]{2,0,1:T(8,128)S(1)}, u32[]{:S(2)}, u32[]{:S(2)}) async-start(f32[8,32,512]{2,0,1:T(8,128)} %copy.112), calls=%async_computation.3 | async-start | bytes 1048576 | tf_op jit(solution)/shard_map/all_to_all | solution.py:159
  277.2 20.7 %all-to-all-start.4 = ((f32[256,4,128]{2,1,0:T(4,128)}), f32[256,4,128]{2,1,0:T(4,128)S(1)}, u32[]{:S(2)}, u32[]{:S(2)}) async-start(f32[256,4,128]{2,1,0:T(4,128)} %param.12), calls=%async_computation.4 | async-start | bytes 1048576 | tf_op jit(solution)/shard_map/all_to_all | solution.py:172
  286.4 172.5 %all-reduce.3.cloned.1.call-start = ((), (), s32[]{:S(2)}) async-start(), calls=%async_computation.6 | async-start | bytes 262144 | tf_op jit(solution)/shard_map/psum | solution.py:180
  286.5 4.8 collective-permute-start
  288.7 6.4 %collective-permute-start.1 = (f32[8,1,4096]{2,0,1:T(8,128)S(1)}, f32[8,1,4096]{2,0,1:T(8,128)S(1)}, u32[]{:S(2)}, u32[]{:S(2)}) collective-permute-start(f32[8,1,4096]{2,0,1:T(8,128)S(1)} %get-tuple-element.85), channel_id=1, source_target_pairs={{32,0},{64,32},{96,64},{128,96},{160,128},{192,160},{224,192},{33,... | collective-permute-start | bytes 393224 | tf_op jit(solution)/shard_map/ppermute | solution.py:23
  334.7 18.1 %copy-start.5 = (bf16[4,128,128]{2,1,0:T(8,128)(2,1)S(1)}, bf16[4,128,128]{2,1,0:T(8,128)(2,1)}, u32[]{:S(2)}) copy-start(bf16[4,128,128]{2,1,0:T(8,128)(2,1)} %param.13) | copy-start | bytes 393220
  346.0 275.7 %copy-start.1 = (f32[8,4,128,128]{3,2,1,0:T(8,128)S(1)}, f32[8,4,128,128]{3,2,1,0:T(8,128)}, u32[]{:S(2)}) copy-start(f32[8,4,128,128]{3,2,1,0:T(8,128)} %param.14) | copy-start | bytes 6291460
  353.8 239.7 %all-reduce.5.cloned.1.call-start = ((), (), s32[]{:S(2)}) async-start(), calls=%async_computation.7 | async-start | bytes 131072 | tf_op jit(solution)/shard_map/psum | solution.py:183
  484.5 1.5 copy-start.3
Sparse Core Ops, SparseCore 0:
  353.9 104.9 all-reduce.2
  486.1 107.3 all-reduce.4
where the time goes:
time: 633 us; the launch traced here: 629 us
  waiting for transfers between devices  264 us (42%)
  local copies, waits for them, and re-layouts  170 us (27%)
  blocking collectives  73.1 us (12%)
  matrix products  49.3 us (8%)
  other arithmetic  34.9 us (6%)
  starting transfers between devices  20 us (3%)
  between operations  17.3 us (3%)
    unnamed x30, local copies, waits for them, and re-layouts  118 us
    psum x1, waiting for transfers between devices, on_device(): lax.psum(jnp.einsum('krw,jrw->kj', coords, coords, precision=hi), 'chan')  106 us
    psum x1, waiting for transfers between devices, on_device(): sketch = lax.psum(take_sketch(pixels, sketch_rows), 'chan')  105 us
    all_to_all x1, blocking collectives, data_gradient(): lax.all_to_all(inverted, 'facet', split_axis=3, concat_axis=2, tiled=True)  30.5 us
    dot_general x78, matrix products, matmul_hi(): return jnp.dot(first_mat, second_mat, precision=lax.Precision.HIGHEST)  29.9 us
    all_to_all x1, waiting for transfers between devices, data_gradient(): lax.all_to_all(column_spec, 'facet', split_axis=2, concat_axis=3, tiled=T...  28.5 us
    all_to_all x1, blocking collectives, data_gradient(): lax.all_to_all(sky_image, 'facet', split_axis=2, concat_axis=1, tiled=True)  25.4 us
    all_to_all x1, blocking collectives, on_device(): lax.all_to_all(merged, 'chan', split_axis=2, concat_axis=0, tiled=True)  17.2 us
  transfers between devices with their start and end apart: 7, of which 7 were waited for; matrix products, arithmetic and copies ran while one was open for 0% of the time, Pallas kernels for 0%

commit v1 on v0

--- a/solution.py
+++ b/solution.py
@@ -180,7 +180,9 @@
     sketch = lax.psum(take_sketch(pixels, sketch_rows), "chan")
     basis_mat = basis_from(sketch)
     coords = project_rows(basis_mat, pixels)
-    gram_mat = lax.psum(jnp.einsum("krw,jrw->kj", coords, coords, precision=hi), "chan")
+    part = jnp.einsum("krw,jrw->kj", coords, coords, precision=hi)
+    pieces = lax.all_gather(part, "chan", axis=0, tiled=False)
+    gram_mat = pieces.sum(axis=0)
     shrink = shrink_matrix(gram_mat)
     new_dual = pixels - jnp.einsum(
         "ck,krw->crw", matmul_hi(basis_mat, shrink), coords, precision=hi

time: 633 us -> 571 us (0.902)
  waiting for transfers between devices: 264 us -> 205 us
    psum x1 -> x0, waiting for transfers between devices: 106 us -> none  [on_device(): lax.psum(jnp.einsum('krw,jrw->kj', coords, coords, precision=hi), 'chan')]
    all_gather x0 -> x1, waiting for transfers between devices: none -> 47.7 us  [on_device(): pieces = lax.all_gather(part, 'chan', axis=0, tiled=False)]
    unnamed x30 -> x32, local copies, waits for them, and re-layouts: 118 us -> 118 us
where the time goes in v1:
time: 571 us; the launch traced here: 567 us
  waiting for transfers between devices  205 us (36%)
  local copies, waits for them, and re-layouts  169 us (30%)
  blocking collectives  73 us (13%)
  matrix products  47.6 us (8%)
  other arithmetic  33.9 us (6%)
  starting transfers between devices  19.9 us (3%)
  between operations  17.1 us (3%)
    unnamed x32, local copies, waits for them, and re-layouts  118 us
    psum x1, waiting for transfers between devices, on_device(): sketch = lax.psum(take_sketch(pixels, sketch_rows), 'chan')  105 us
    all_gather x1, waiting for transfers between devices, on_device(): pieces = lax.all_gather(part, 'chan', axis=0, tiled=False)  47.7 us
    all_to_all x1, blocking collectives, data_gradient(): lax.all_to_all(inverted, 'facet', split_axis=3, concat_axis=2, tiled=True)  30.5 us
    all_to_all x1, waiting for transfers between devices, data_gradient(): lax.all_to_all(column_spec, 'facet', split_axis=2, concat_axis=3, tiled=T...  28.5 us
    dot_general x78, matrix products, matmul_hi(): return jnp.dot(first_mat, second_mat, precision=lax.Precision.HIGHEST)  28.2 us
    all_to_all x1, blocking collectives, data_gradient(): lax.all_to_all(sky_image, 'facet', split_axis=2, concat_axis=1, tiled=True)  25.4 us
    all_to_all x1, blocking collectives, on_device(): lax.all_to_all(merged, 'chan', split_axis=2, concat_axis=0, tiled=True)  17.2 us
  transfers between devices with their start and end apart: 7, of which 7 were waited for; matrix products, arithmetic and copies ran while one was open for 0% of the time, Pallas kernels for 0%

profile of v1, /device:TPU:1, one launch (start us, length us, event | category | flops | bytes accessed | tf_op | source)
XLA Modules:
  0.0 567.0 jit_solution(2938320533680479425)
XLA Ops:
  7.2 6.9 %copy.95 = f32[8,4,4096]{0,1,2:T(4,128)} copy(f32[8,4,4096]{2,1,0:T(4,128)} %param.11) | data formatting | bytes 1048576 | tf_op args[0]
  14.1 11.4 %reshape.87 = f32[8,1,16384]{2,1,0:T(1,128)S(1)} reshape(f32[4096,4,8]{2,1,0:T(4,128)} %bitcast.219) | data formatting | bytes 1048576
  25.5 25.4 %all_to_all.105 = f32[8,1,16384]{2,1,0:T(1,128)S(1)} all-to-all(f32[8,1,16384]{2,1,0:T(1,128)S(1)} %reshape.87), channel_id=1, replica_groups=mesh['facet'=8,'chan'=32] {'facet'}, dimensions={0} | all-to-all | bytes 1048576 | tf_op jit(solution)/shard_map/all_to_all | solution.py:123
  53.3 13.1 %reshape.88 = f32[4096,4,8]{2,1,0:T(4,128)} reshape(f32[8,16384]{1,0:T(8,128)S(1)} %reduce.6) | data formatting | bytes 1048576
  66.4 6.7 %copy.96 = f32[8,4,8,512]{3,1,2,0:T(4,128)S(1)} copy(f32[8,4,8,512]{0,1,3,2:T(4,128)} %bitcast.216) | data formatting | bytes 1048576 | tf_op jit(solution)/shard_map/all_to_all | solution.py:123
  80.4 28.5 %all-to-all-done.1 = f32[8,2,32,512]{3,0,1,2:T(8,128)S(1)} async-done(((f32[8,2,32,512]{3,0,1,2:T(8,128)}), f32[8,2,32,512]{3,0,1,2:T(8,128)S(1)}, u32[]{:S(2)}, u32[]{:S(2)}) %all-to-all-start.1) | async-done | bytes 1048608 | tf_op jit(solution)/shard_map/all_to_all | solution.py:130
  135.1 11.1 %copy.110 = f32[2,8,4,4096]{1,2,0,3:T(4,128)} copy(f32[2,8,4,4096]{3,2,1,0:T(4,128)S(1)} %mul.315) | data formatting | bytes 2097152 | tf_op jit(solution)/shard_map/mul | solution.py:114
  146.2 14.5 %bitcast_bitcast_fusion = f32[4096,2,4,8]{3,2,1,0:T(4,128)} fusion(f32[2,8,4,4096]{1,2,0,3:T(4,128)} %copy.110), kind=kLoop, calls=%fused_computation.239 | loop fusion | bytes 2097152
  160.6 21.3 %reshape.89 = f32[8,1,32768]{2,1,0:T(1,128)S(1)} reshape(f32[4096,2,4,8]{3,2,1,0:T(4,128)} %bitcast_bitcast_fusion) | data formatting | bytes 2097152
  181.9 30.5 %all_to_all.106 = f32[8,1,32768]{2,1,0:T(1,128)S(1)} all-to-all(f32[8,1,32768]{2,1,0:T(1,128)S(1)} %reshape.89), channel_id=1, replica_groups=mesh['facet'=8,'chan'=32] {'facet'}, dimensions={0} | all-to-all | bytes 2097152 | tf_op jit(solution)/shard_map/all_to_all | solution.py:154
  215.6 25.6 %reshape.90 = f32[4096,2,4,8]{3,2,1,0:T(4,128)} reshape(f32[8,32768]{1,0:T(8,128)S(1)} %reduce.7) | data formatting | bytes 2097152
  241.2 13.2 %copy.111 = f32[8,2,4,8,512]{4,2,3,0,1:T(4,128)S(1)} copy(f32[8,2,4,8,512]{0,2,1,4,3:T(4,128)} %bitcast.215) | data formatting | bytes 2097152 | tf_op jit(solution)/shard_map/all_to_all | solution.py:154
  261.0 16.0 %all-to-all-done.3 = f32[8,32,512]{2,0,1:T(8,128)S(1)} async-done(((f32[8,32,512]{2,0,1:T(8,128)}), f32[8,32,512]{2,0,1:T(8,128)S(1)}, u32[]{:S(2)}, u32[]{:S(2)}) %all-to-all-start.3) | async-done | bytes 524320 | tf_op jit(solution)/shard_map/all_to_all | solution.py:159
  277.0 9.1 %all-to-all-start.4 = ((f32[256,4,128]{2,1,0:T(4,128)}), f32[256,4,128]{2,1,0:T(4,128)S(1)}, u32[]{:S(2)}, u32[]{:S(2)}) async-start(f32[256,4,128]{2,1,0:T(4,128)} %param.12), calls=%async_computation.4 | async-start | bytes 1048576 | tf_op jit(solution)/shard_map/all_to_all | solution.py:172
  298.0 5.9 %copy.122 = f32[8,4,4096]{0,1,2:T(4,128)} copy(f32[8,4,4096]{2,0,1:T(8,128)S(1)} %get-tuple-element.76) | data formatting | bytes 1048576 | tf_op jit(solution)/shard_map/add | solution.py:177
  303.9 11.4 %reshape.91 = f32[32,1,4096]{2,1,0:T(1,128)S(1)} reshape(f32[4096,4,8]{2,1,0:T(4,128)} %bitcast.217) | data formatting | bytes 1048576
  315.4 17.2 %all_to_all.107 = f32[32,1,4096]{2,1,0:T(1,128)S(1)} all-to-all(f32[32,1,4096]{2,1,0:T(1,128)S(1)} %reshape.91), channel_id=1, replica_groups=mesh['facet'=8,'chan'=32] {'chan'}, dimensions={0} | all-to-all | bytes 1048576 | tf_op jit(solution)/shard_map/all_to_all | solution.py:179
  334.4 11.3 %reshape.92 = f32[4096,4,8]{2,1,0:T(4,128)} reshape(f32[32,4096]{1,0:T(8,128)S(1)} %reduce.8) | data formatting | bytes 1048576
  345.7 6.6 %copy.123 = f32[8,4,32,128]{3,0,2,1:T(8,128)S(1)} copy(f32[8,4,32,128]{0,1,3,2:T(4,128)} %bitcast.218) | data formatting | bytes 1048576 | tf_op jit(solution)/shard_map/all_to_all | solution.py:179
  353.4 105.1 %all-reduce.2.cloned.1.call-done = f32[256,128]{1,0:T(8,128)} async-done(((f32[256,128]{1,0:T(8,128)}), f32[256,128]{1,0:T(8,128)}) %all-reduce.2.cloned.1.call-update) | async-done | bytes 131088 | tf_op jit(solution)/shard_map/psum | solution.py:180
  460.1 11.7 %cholesky.22 = f32[128,128]{1,0:T(8,128)S(1)} custom-call(f32[128,128]{1,0:T(8,128)S(1)} %fusion.62), custom_call_target="Cholesky" | custom-call | tf_op jit(solution)/shard_map/jit(cholesky)/cholesky | solution.py:58
  473.2 9.8 %custom-call.7 = f32[1,128,128]{1,2,0:T(8,128)S(1)} custom-call(f32[1,128,128]{2,1,0:T(8,128)S(1)} %fusion.56), custom_call_target="InvertDiagBlocksLowerTriangular" | custom-call | tf_op jit(solution)/shard_map/jit(_solve_triangular)/triangular_solve | solution.py:59
  486.8 47.7 %all-gather.3.cloned.1.call-done = f32[4096,128]{1,0:T(8,128)} async-done(((f32[128,128]{1,0:T(8,128)}), f32[4096,128]{1,0:T(8,128)}) %all-gather.3.cloned.1.call-update) | async-done | bytes 2097168 | tf_op jit(solution)/shard_map/all_gather | solution.py:184
  546.0 11.4 %while.24 = (s32[]{:T(128)}, f32[128,128]{0,1:T(8,128)S(1)}, f32[128,128]{1,0:T(8,128)S(1)}, s32[]{:T(128)}) while((s32[]{:T(128)}, f32[128,128]{0,1:T(8,128)S(1)}, f32[128,128]{1,0:T(8,128)S(1)}, s32[]{:T(128)}) %tuple.57), condition=%wide.region_10.11_spmd.clone, body=%wide.region_9.10_spmd.clone.sunk | while | flops 75563008 | bytes 852021 | solution.py:52
  (204 shorter events, 94.4 us)
Async XLA Ops:
  7.2 112.7 %copy-start = (f32[8,4,128,128]{3,2,1,0:T(8,128)S(1)}, f32[8,4,128,128]{3,2,1,0:T(8,128)}, u32[]{:S(2)}) copy-start(f32[8,4,128,128]{3,2,1,0:T(8,128)} %param.14) | copy-start | bytes 6291460
  66.4 13.8 %copy-start.7 = (s32[8,4]{0,1:T(4,128)S(1)}, s32[8,4]{0,1:T(4,128)}, u32[]{:S(2)}) copy-start(s32[8,4]{0,1:T(4,128)} %param.15) | copy-start | bytes 388
  66.4 13.8 %copy-start.8 = (s32[8,4]{0,1:T(4,128)S(1)}, s32[8,4]{0,1:T(4,128)}, u32[]{:S(2)}) copy-start(s32[8,4]{0,1:T(4,128)} %param.16) | copy-start | bytes 388
  76.4 32.5 %all-to-all-start.1 = ((f32[8,2,32,512]{3,0,1,2:T(8,128)}), f32[8,2,32,512]{3,0,1,2:T(8,128)S(1)}, u32[]{:S(2)}, u32[]{:S(2)}) async-start(f32[8,2,32,512]{3,0,1,2:T(8,128)} %copy.99), calls=%async_computation.1 | async-start | bytes 2097152 | tf_op jit(solution)/shard_map/all_to_all | solution.py:130
  114.2 7.5 %copy-start.5 = (f32[8,2,4,4,128]{4,3,2,1,0:T(4,128)S(1)}, f32[8,2,4,4,128]{4,3,2,1,0:T(4,128)}, u32[]{:S(2)}) copy-start(f32[8,2,4,4,128]{4,3,2,1,0:T(4,128)} %param.17) | copy-start | bytes 393220
  241.2 19.6 %copy-start.2 = (f32[8,4,4096]{2,1,0:T(4,128)S(1)}, f32[8,4,4096]{2,1,0:T(4,128)}, u32[]{:S(2)}) copy-start(f32[8,4,4096]{2,1,0:T(4,128)} %param.11) | copy-start | bytes 1572868
  257.2 19.8 %all-to-all-start.3 = ((f32[8,32,512]{2,0,1:T(8,128)}), f32[8,32,512]{2,0,1:T(8,128)S(1)}, u32[]{:S(2)}, u32[]{:S(2)}) async-start(f32[8,32,512]{2,0,1:T(8,128)} %copy.112), calls=%async_computation.3 | async-start | bytes 1048576 | tf_op jit(solution)/shard_map/all_to_all | solution.py:159
  277.0 20.6 %all-to-all-start.4 = ((f32[256,4,128]{2,1,0:T(4,128)}), f32[256,4,128]{2,1,0:T(4,128)S(1)}, u32[]{:S(2)}, u32[]{:S(2)}) async-start(f32[256,4,128]{2,1,0:T(4,128)} %param.12), calls=%async_computation.4 | async-start | bytes 1048576 | tf_op jit(solution)/shard_map/all_to_all | solution.py:172
  286.2 172.3 %all-reduce.2.cloned.1.call-start = ((), (), s32[]{:S(2)}) async-start(), calls=%async_computation.6 | async-start | bytes 262144 | tf_op jit(solution)/shard_map/psum | solution.py:180
  286.2 4.8 collective-permute-start
  288.5 6.4 %collective-permute-start.1 = (f32[8,1,4096]{2,0,1:T(8,128)S(1)}, f32[8,1,4096]{2,0,1:T(8,128)S(1)}, u32[]{:S(2)}, u32[]{:S(2)}) collective-permute-start(f32[8,1,4096]{2,0,1:T(8,128)S(1)} %get-tuple-element.85), channel_id=1, source_target_pairs={{32,0},{64,32},{96,64},{128,96},{160,128},{192,160},{224,192},{33,... | collective-permute-start | bytes 393224 | tf_op jit(solution)/shard_map/ppermute | solution.py:23
  334.4 17.9 %copy-start.6 = (bf16[4,128,128]{2,1,0:T(8,128)(2,1)S(1)}, bf16[4,128,128]{2,1,0:T(8,128)(2,1)}, u32[]{:S(2)}) copy-start(bf16[4,128,128]{2,1,0:T(8,128)(2,1)} %param.13) | copy-start | bytes 393220
  353.4 181.1 %all-gather.3.cloned.1.call-start = ((), (), s32[]{:S(2)}) async-start(), calls=%async_computation.7 | async-start | bytes 2162688 | tf_op jit(solution)/shard_map/all_gather | solution.py:184
  458.5 101.3 %copy-start.1 = (f32[8,4,128,128]{3,2,1,0:T(8,128)S(1)}, f32[8,4,128,128]{3,2,1,0:T(8,128)}, u32[]{:S(2)}) copy-start(f32[8,4,128,128]{3,2,1,0:T(8,128)} %param.14) | copy-start | bytes 6291460
  484.2 1.5 copy-start.3
  486.8 70.8 %copy-start.4 = (f32[128,256]{1,0:T(8,128)S(1)}, f32[128,256]{1,0:T(8,128)}, u32[]{:S(2)}) copy-start(f32[128,256]{1,0:T(8,128)} %copy-done.3) | copy-start | bytes 393220
Sparse Core Ops, SparseCore 0:
  353.5 104.9 all-reduce.1
  485.8 48.6 all-gather.2
